TPU v7x, 128 devices: a whole 4x4x4 slice. The times are simulated.
128 devices in a mesh: page: 8 (over z, core), tensor: 16 (over x, y).
Axes of the slice: x: 4, y: 4, z: 4, core: 2. Of those that a mesh axis runs over, the one named last changes fastest.
Arguments:
- hidden_in: bfloat16 [1, 32, 8192], P(None, 'tensor', 'page'), may hold values from -6 to 6
- w_query: bfloat16 [8192, 8192], P('page', 'tensor'), may hold values from -0.0625 to 0.0625
- w_keyval: bfloat16 [8192, 2048], P('page', 'tensor'), may hold values from -0.0625 to 0.0625
- w_output: bfloat16 [8192, 8192], P('tensor', 'page'), may hold values from -0.0625 to 0.0625
- kv_pool: bfloat16 [8192, 64, 2048], P(('page', 'tensor'))
- page_table: int32 [8192], replicated, may hold values from 0 to 8191, each once
- selected: int32 [1, 32, 8, 32], replicated, may hold values from 0 to 255, as said below
Outputs:
- attn_out: bfloat16 [1, 32, 8192], P(None, 'tensor', 'page')
- new_kv: bfloat16 [1, 32, 2048], P(None, 'page', 'tensor')
Inputs may be any that keep to these rules, and one draw needn't show every extreme that they name: `page_table`: each pool slot holds exactly one page: entry s * 256 + l is the slot of page l of sequence s. `selected`: the 32 pages of one row are different.
All inputs are finite; a program needn't handle non-finite values.
Results may differ from a plain program's by a relative error of at most 0.018.
The roundings to bfloat16 on the way count: a program that leaves them out, or rounds other values in their place, can miss the bound.
Values may be sent and summed in bfloat16 or wider, within the bound.
No kernel may reach another device: no remote copies, remote signals or barrier semaphores. Data moves between devices by JAX's collectives and lax.ppermute only.
A program may use at most 192 MiB of HBM per device.

v0:
```python
import math
import jax
import jax.numpy as jnp
from jax import lax
from jax.sharding import PartitionSpec as P

H = 64
KVH = 8
HD = 128
PAGE_TOK = 64
PAGES = 256
NEG_BIG = -1e30


def frequencies(head_dim):
    half_dim = head_dim // 2
    index = jnp.arange(half_dim, dtype=jnp.float32)
    base_freq = jnp.exp(-(2.0 * index / head_dim) * math.log(500000.0))
    wavelen = 2.0 * math.pi / base_freq
    smooth = (8192.0 / wavelen - 1.0) / 3.0
    middle = (1.0 - smooth) * base_freq / 8.0 + smooth * base_freq
    scaled = jnp.where(wavelen > 8192.0, base_freq / 8.0, base_freq)
    is_middle = jnp.logical_and(wavelen >= 2048.0, wavelen <= 8192.0)
    return jnp.where(is_middle, middle, scaled)


def rotate(vectors, position):
    half_dim = vectors.shape[-1] // 2
    angles = position * frequencies(vectors.shape[-1])
    cosine = jnp.cos(angles)
    sine_v = jnp.sin(angles)
    first_half = vectors[..., :half_dim]
    second_half = vectors[..., half_dim:]
    return jnp.concatenate(
        [first_half * cosine - second_half * sine_v, first_half * sine_v + second_half * cosine],
        axis=-1,
    )


def finish(summed, position, query_cols, kind_ids):
    n_rows = summed.shape[0]
    query = rotate(summed[:, :query_cols].reshape(n_rows, query_cols // HD, HD), position)
    query = query.reshape(n_rows, query_cols).astype(jnp.bfloat16)
    keyval = summed[:, query_cols:].reshape(n_rows, -1, HD)
    rotated = rotate(keyval, position)
    keyval = jnp.where(kind_ids[None, :, None] == 0, rotated, keyval)
    return (query, keyval.reshape(n_rows, -1).astype(jnp.bfloat16))


def per_device(hidden_in, w_query, w_keyval, w_output, kv_pool, page_table, selected):
    n_page = lax.axis_size("page")
    n_tensor = lax.axis_size("tensor")
    my_page = lax.axis_index("page")
    my_tensor = lax.axis_index("tensor")
    seqs = selected.shape[1]
    groups = H // KVH
    local_heads = H // n_tensor
    scale = 1.0 / math.sqrt(HD)
    slots = kv_pool.shape[0]
    pool_size = page_table.shape[0]
    device = my_page * n_tensor + my_tensor
    logical = (
        jnp.zeros((pool_size,), jnp.int32)
        .at[page_table]
        .set(jnp.arange(pool_size, dtype=jnp.int32))
    )
    my_logical = lax.dynamic_slice_in_dim(logical, device * slots, slots)
    seq_of = my_logical // PAGES
    page_of = my_logical % PAGES
    owner_rows = jnp.arange(seqs, dtype=jnp.int32)[:, None] == seq_of[None, :]
    owner_hot = owner_rows.astype(jnp.float32)
    w_joined = jnp.concatenate([w_query, w_keyval], axis=1)
    query_cols = w_query.shape[1]
    sub_heads = w_keyval.shape[1] // HD
    kind_ids = (my_tensor * sub_heads + jnp.arange(sub_heads, dtype=jnp.int32)) % 2
    pool_five = kv_pool.reshape(slots, PAGE_TOK, KVH, 2, HD)
    key_rows = pool_five[:, :, :, 0]
    val_rows = pool_five[:, :, :, 1]
    seq_share = seqs // n_page
    position = float(PAGES * PAGE_TOK)
    tok_rows = hidden_in[0]
    partial_value = jnp.dot(
        lax.all_gather(tok_rows, "tensor", axis=0, tiled=True),
        w_joined,
        preferred_element_type=jnp.float32,
    )
    summed = lax.psum(partial_value, "page")
    query, new_local = finish(summed, position, query_cols, kind_ids)
    new_rows = [lax.dynamic_slice_in_dim(new_local, my_page * seq_share, seq_share, 0)]
    query_full = lax.all_gather(query, "tensor", axis=1, tiled=True)
    sel_rows = selected[0][seq_of]
    picked = jnp.any(sel_rows == page_of[:, None, None], axis=2)
    slot_query = query_full[seq_of].reshape(slots, KVH, groups, HD)
    scores = (
        jnp.einsum("sghd,stgd->sght", slot_query, key_rows, preferred_element_type=jnp.float32)
        * scale
    )
    page_max = jnp.max(scores, axis=-1)
    weights = jnp.exp(scores - page_max[..., None]).astype(jnp.bfloat16)
    pick_mask = picked.astype(jnp.float32)[:, :, None]
    page_total = jnp.sum(weights.astype(jnp.float32), axis=-1) * pick_mask
    weighted = (
        jnp.einsum("sght,stgd->sghd", weights, val_rows, preferred_element_type=jnp.float32)
        * pick_mask[..., None]
    )
    page_max = jnp.where(picked[:, :, None], page_max, NEG_BIG)
    seq_max = jnp.max(jnp.where(owner_rows[:, :, None, None], page_max[None], NEG_BIG), axis=1)
    factor = jnp.exp(page_max - seq_max[seq_of])
    seq_total = jnp.dot(
        owner_hot, (page_total * factor).reshape(slots, H), precision=lax.Precision.HIGHEST
    )
    seq_acc = jnp.dot(
        owner_hot,
        (weighted * factor[..., None]).reshape(slots, H * HD),
        precision=lax.Precision.HIGHEST,
    ).reshape(seqs, H, HD)
    seq_max = seq_max.reshape(seqs, H)
    top_max = lax.pmax(seq_max, ("page", "tensor"))
    rescale = jnp.exp(seq_max - top_max)
    full_total, full_acc = lax.psum(
        (seq_total * rescale, seq_acc * rescale[..., None]), ("page", "tensor")
    )
    head_start = my_tensor * local_heads
    mine_total = lax.dynamic_slice_in_dim(full_total, head_start, local_heads, 1)
    mine_acc = lax.dynamic_slice_in_dim(full_acc, head_start, local_heads, 1)
    heads = (mine_acc / mine_total[..., None]).astype(jnp.bfloat16).reshape(seqs, local_heads * HD)
    outputs = [
        lax.psum_scatter(
            jnp.dot(heads, w_output, preferred_element_type=jnp.float32),
            "tensor",
            scatter_dimension=0,
            tiled=True,
        ).astype(jnp.bfloat16)
    ]
    return (jnp.stack(outputs), jnp.stack(new_rows))


def solution(mesh):
    return jax.shard_map(
        per_device,
        mesh=mesh,
        in_specs=(
            P(None, "tensor", "page"),
            P("page", "tensor"),
            P("page", "tensor"),
            P("tensor", "page"),
            P(("page", "tensor"), None, None),
            P(),
            P(),
        ),
        out_specs=(P(None, "tensor", "page"), P(None, "page", "tensor")),
        check_vma=False,
    )
```

profile of v0, /device:TPU:0, one launch (start us, length us, event | category | flops | bytes accessed | tf_op | source)
XLA Modules:
  0.0 482.4 jit_solution(10256855988019674995)
XLA Ops:
  7.2 0.8 copy.29
  8.0 24.1 %all-gather = bf16[1,32,1024]{2,0,1:T(2,128)(2,1)S(1)} all-gather(bf16[1,2,1024]{2,0,1:T(2,128)(2,1)S(1)} %copy.29), channel_id=2, replica_groups=mesh['page'=8,'tensor'=16] {'tensor'}, dimensions={1}, use_global_device_ids=true | all-gather | bytes 69632 | tf_op jit(solution)/shard_map/all_gather | solution.py:83
  32.1 2.3 fusion.12
  34.5 30.5 %scatter_custom_fusion = s32[8192]{0:T(1024)S(1)} fusion(s32[8192]{0:T(1024)S(1)} %compare_select_fusion, s32[8192]{0:T(1024)S(1)} %iota.30, s32[]{:T(128)} %constant.80.clone.1), kind=kCustom, calls=%fused_computation.46 | custom fusion | bytes 32772 | tf_op jit(solution)/shard_map/scatter | solution.py:65
  65.2 27.4 %reshape.97 = bf16[64,64,8,2,128]{4,3,2,1,0:T(2,128)(2,1)} reshape(bf16[64,64,2048]{2,1,0:T(8,128)(2,1)} %param.11) | data formatting | bytes 33554432 | tf_op jit(solution)/shard_map/reshape | solution.py:76
  92.6 33.7 %fusion.37 = (bf16[64,64,8,1,128]{4,3,2,1,0:T(2,128)(2,1)}, bf16[64,64,8,1,128]{4,3,2,1,0:T(2,128)(2,1)}) fusion(bf16[64,64,8,2,128]{4,3,2,1,0:T(2,128)(2,1)} %reshape.97), kind=kLoop, calls=%fused_computation.74 | loop fusion | bytes 33554432 | tf_op jit(solution)/shard_map/slice | solution.py:78
  126.3 0.6 gather_fusion.1
  126.9 1.3 compare_reduce_fusion
  128.3 0.6 convert_element_type.33
  130.1 0.8 slice.38
  131.2 23.4 %all_gather.7 = bf16[32,8192]{1,0:T(8,128)(2,1)S(1)} all-gather(bf16[32,512]{1,0:T(8,128)(2,1)S(1)} %bitcast.76), channel_id=1, replica_groups=mesh['page'=8,'tensor'=16] {'tensor'}, dimensions={1}, use_global_device_ids=true | all-gather | bytes 557056 | tf_op jit(solution)/shard_map/all_gather | solution.py:90
  154.6 1.2 gather_fusion
  156.1 10.3 %multiply_reduce_fusion = (f32[64,8,8]{2,1,0:T(8,128)S(1)}, f32[64,8,8,64]{3,2,1,0:T(8,128)S(1)}) fusion(bf16[64,8,8,128]{3,2,1,0:T(8,128)(2,1)S(1)} %bitcast.70, bf16[64,64,8,1,128]{4,3,2,1,0:T(2,128)(2,1)} %get-tuple-element.9), kind=kOutput, calls=%fused_computation.15 | convolution fusion | flops 67629056 | bytes 10502144 | tf_op jit(solution)/shard_map/sghd,stgd->sght/dot_general | solution.py:95
  166.4 0.8 broadcast_select_fusion
  167.3 1.7 copy.32
  168.9 1.1 select_reduce_fusion
  170.0 0.7 copy.34
  170.8 1.4 gather_fusion.2
  172.2 2.0 convert_reduce_fusion
  174.2 64.2 %pmax.7 = f32[32,64]{0,1:T(8,128)S(1)} all-reduce(f32[32,64]{0,1:T(8,128)S(1)} %bitcast.74), channel_id=1, replica_groups=mesh['page'=8,'tensor'=16] {'page','tensor'}, use_global_device_ids=true, to_apply=%region_5.6 | all-reduce | flops 2048 | bytes 16384 | tf_op jit(solution)/shard_map/pmax | solution.py:118
  238.4 2.0 multiply_multiply_fusion.1
  240.4 1.1 copy.35
  241.5 9.7 %multiply_multiply_fusion = f32[64,8,8,128]{3,2,1,0:T(8,128)S(1)} fusion(bf16[64,64,8,1,128]{4,3,2,1,0:T(2,128)(2,1)} %get-tuple-element.8, f32[64,8,8]{2,1,0:T(8,128)} %get-tuple-element.3, f32[64,8]{1,0:T(8,128)S(1)} %copy-done.3, f32[64,8,8,64]{3,2,1,0:T(8,128)S(1)} %get-tuple-element.15, f32[64,8,8]{2,1,0:T(8,128)S(1)} %get-tuple-element.14), kind=kOutput, calls=%fused_computation.13 | convolution fusion | flops 68943872 | bytes 11569152 | tf_op jit(solution)/shard_map/sght,stgd->sghd/dot_general | solution.py:103
  251.4 3.2 fusion.5
  254.6 0.7 slice_bitcast_fusion
  255.3 0.7 slice.43
  256.0 65.0 %psum.23 = f32[32,64]{0,1:T(8,128)S(1)} all-reduce(f32[32,64]{0,1:T(8,128)S(1)} %convolution_multiply_fusion), channel_id=1, replica_groups=mesh['page'=8,'tensor'=16] {'page','tensor'}, use_global_device_ids=true, to_apply=%region_8.9 | all-reduce | flops 2048 | bytes 16384 | tf_op jit(solution)/shard_map/psum | solution.py:120
  321.1 0.6 fusion.31
  321.8 78.1 %all-reduce.7.cloned.1.call-done = f32[32,64,128]{2,0,1:T(8,128)} async-done(((f32[32,64,128]{2,0,1:T(8,128)}), f32[32,64,128]{2,0,1:T(8,128)}) %all-reduce.7.cloned.1.call-update) | async-done | bytes 1048592 | tf_op jit(solution)/shard_map/psum | solution.py:120
  399.9 1.2 fusion.17
  401.0 73.9 %all-reduce.8 = bf16[32,1024]{1,0:T(8,128)(2,1)S(1)} all-reduce(f32[32,1024]{1,0:T(8,128)S(1)} %fusion.17), channel_id=3, replica_groups=mesh['page'=8,'tensor'=16] {'tensor'}, use_global_device_ids=true, to_apply=%region_9.10.clone | all-reduce | flops 32768 | bytes 196608
  475.0 0.6 fusion.27
  (44 shorter events, 1.8 us)
Async XLA Ops:
  7.2 392.7 %copy-start = (bf16[512,1024]{1,0:T(8,128)(2,1)S(1)}, bf16[512,1024]{1,0:T(8,128)(2,1)}, u32[]{:S(2)}) copy-start(bf16[512,1024]{1,0:T(8,128)(2,1)} %param.10) | copy-start | bytes 3145732
  7.2 27.3 %copy-start.4 = (s32[8192]{0:T(1024)S(1)}, s32[8192]{0:T(1024)}, u32[]{:S(2)}) copy-start(s32[8192]{0:T(1024)} %param.12) | copy-start | bytes 98308
  7.2 122.9 %all-reduce.5.cloned.1.call-start = ((), (), s32[]{:S(2)}) async-start(), calls=%async_computation | async-start | bytes 163840 | tf_op jit(solution)/shard_map/psum | solution.py:87
  34.4 365.4 %all-reduce.7.cloned.1.call-start = ((), (), s32[]{:S(2)}) async-start(), calls=%async_computation.1 | async-start | bytes 2097152 | tf_op jit(solution)/shard_map/psum | solution.py:120
  65.2 89.4 %copy-start.5 = (s32[1024]{0:T(1024)}, s32[1024]{0:T(1024)S(1)}, u32[]{:S(2)}) copy-start(s32[1024]{0:T(1024)S(1)} %pad_clamp_fusion) | copy-start | bytes 12292
  92.6 33.7 %copy-start.1 = (s32[1,32,8,32]{3,2,1,0:T(8,128)S(1)}, s32[1,32,8,32]{3,2,1,0:T(8,128)}, u32[]{:S(2)}) copy-start(s32[1,32,8,32]{3,2,1,0:T(8,128)} %param.13) | copy-start | bytes 98308
  92.6 36.3 %copy-start.10 = (u32[128]{0:T(128)S(1)}, u32[128]{0:T(128)}, u32[]{:S(2)}) copy-start(u32[128]{0:T(128)} %constant.117) | copy-start | bytes 1540
  128.2 27.6 %copy-start.6 = (f32[64]{0:T(128)}, f32[64]{0:T(128)S(1)}, u32[]{:S(2)}) copy-start(f32[64]{0:T(128)S(1)} %get-tuple-element.16) | copy-start | bytes 772
  128.2 27.6 %copy-start.8 = (f32[64]{0:T(128)}, f32[64]{0:T(128)S(1)}, u32[]{:S(2)}) copy-start(f32[64]{0:T(128)S(1)} %get-tuple-element.17) | copy-start | bytes 772
  172.2 2.0 copy-start.2
  172.2 66.2 %copy-start.3 = (f32[64,8]{1,0:T(8,128)S(1)}, f32[64,8]{1,0:T(8,128)}, u32[]{:S(2)}) copy-start(f32[64,8]{1,0:T(8,128)} %convert_element_type.33) | copy-start | bytes 6148
  251.4 69.6 %copy-start.7 = (f32[64]{0:T(128)S(1)}, f32[64]{0:T(128)}, u32[]{:S(2)}) copy-start(f32[64]{0:T(128)} %copy-done.6) | copy-start | bytes 772
  251.4 69.6 %copy-start.9 = (f32[64]{0:T(128)S(1)}, f32[64]{0:T(128)}, u32[]{:S(2)}) copy-start(f32[64]{0:T(128)} %copy-done.8) | copy-start | bytes 772
Sparse Core Ops, SparseCore 0:
  34.5 55.7 all-reduce.4
  254.7 145.0 all-reduce.6
where the time goes:
time: 484 us; the launch traced here: 482 us
  blocking collectives  251 us (52%)
  local copies, waits for them, and re-layouts  103 us (21%)
  waiting for transfers between devices  78.1 us (16%)
  matrix products  26.8 us (6%)
  between operations  15 us (3%)
  other arithmetic  9.03 us (2%)
    psum x1, waiting for transfers between devices, per_device(): lax.psum((seq_total * rescale, seq_acc * rescale[..., None]), ('page', 't...  78.1 us
    unnamed x1, blocking collectives  73.9 us
    psum x1, blocking collectives, per_device(): lax.psum((seq_total * rescale, seq_acc * rescale[..., None]), ('page', 't...  65 us
    pmax x1, blocking collectives, per_device(): top_max = lax.pmax(seq_max, ('page', 'tensor'))  64.2 us
    slice x1, local copies, waits for them, and re-layouts, per_device(): val_rows = pool_five[:, :, :, 1]  33.7 us
    scatter x1, local copies, waits for them, and re-layouts, per_device(): logical = jnp.zeros((pool_size,), jnp.int32).at[page_table].set(jnp.arang...  30.5 us
    reshape x1, local copies, waits for them, and re-layouts, per_device(): pool_five = kv_pool.reshape(slots, PAGE_TOK, KVH, 2, HD)  27.4 us
    all_gather x1, blocking collectives, per_device(): lax.all_gather(tok_rows, 'tensor', axis=0, tiled=True)  24.1 us
  transfers between devices with their start and end apart: 2, of which 1 were waited for; matrix products, arithmetic and copies ran while one was open for 20% of the time, Pallas kernels for 0%

commit v1 on v0

--- a/solution.py
+++ b/solution.py
@@ -10,6 +10,13 @@
 PAGE_TOK = 64
 PAGES = 256
 NEG_BIG = -1e30
+
+
+def _fill_core(raw, dim_at):
+    g_now = list(raw.shape[1:])
+    g_now[dim_at] *= raw.shape[0]
+    fresh = jnp.moveaxis(raw, 0, dim_at).reshape(g_now)
+    return fresh
 
 
 def frequencies(head_dim):
@@ -87,7 +94,25 @@
     summed = lax.psum(partial_value, "page")
     query, new_local = finish(summed, position, query_cols, kind_ids)
     new_rows = [lax.dynamic_slice_in_dim(new_local, my_page * seq_share, seq_share, 0)]
-    query_full = lax.all_gather(query, "tensor", axis=1, tiled=True)
+    lanes = lax.axis_size("tensor")
+    steps_seen = tuple(((to_i, (to_i + 1) % lanes) for to_i in range(lanes)))
+    trail = tuple(((src_i, nth) for nth, src_i in steps_seen))
+    row_out, extra = ([], [])
+    j = 0
+    while j < lanes - 1:
+        if j % 2 == 0:
+            row_out.append(
+                lax.ppermute(row_out[-1] if row_out else query, axis_name="tensor", perm=steps_seen)
+            )
+        else:
+            extra.append(
+                lax.ppermute(extra[-1] if extra else query, axis_name="tensor", perm=trail)
+            )
+        j = j + 1
+    found_now = jnp.stack([*row_out[::-1], query, *extra], axis=0)
+    odd = lax.axis_index("tensor") - len(row_out)
+    found_now = found_now[(jnp.arange(lanes) - odd) % lanes]
+    query_full = _fill_core(found_now, 1)
     sel_rows = selected[0][seq_of]
     picked = jnp.any(sel_rows == page_of[:, None, None], axis=2)
     slot_query = query_full[seq_of].reshape(slots, KVH, groups, HD)

time: 484 us -> 518 us (1.070)
  starting transfers between devices: 0.08 us -> 39.6 us
  blocking collectives: 251 us -> 230 us
  waiting for transfers between devices: 78.1 us -> 93.2 us
    ppermute x0 -> x15, starting transfers between devices: none -> 39.5 us  [the longest x7 38.2 us: per_device(): lax.ppermute(extra[-1] if extra else query, axis_name='tensor', perm=trail)]
    all_gather x1 -> x0, blocking collectives: 23.4 us -> none  [per_device(): query_full = lax.all_gather(query, 'tensor', axis=1, tiled=True)]
    ppermute x0 -> x15, waiting for transfers between devices: none -> 14.6 us  [the longest x8 11.3 us: per_device(): lax.ppermute(row_out[-1] if row_out else query, axis_name='tensor', perm=...]
  transfers between devices with their start and end apart: 2 -> 17, of which waited for: 1 -> 10; matrix products, arithmetic and copies ran while one was open for 20% -> 19% of each run, Pallas kernels for 0% -> 0%
where the time goes in v1:
time: 518 us; the launch traced here: 516 us
  blocking collectives  230 us (44%)
  local copies, waits for them, and re-layouts  103 us (20%)
  waiting for transfers between devices  93.2 us (18%)
  starting transfers between devices  39.6 us (8%)
  matrix products  26.7 us (5%)
  between operations  15.2 us (3%)
  other arithmetic  9.6 us (2%)
    psum x1, waiting for transfers between devices, per_device(): lax.psum((seq_total * rescale, seq_acc * rescale[..., None]), ('page', 't...  78.5 us
    unnamed x1, blocking collectives  73.9 us
    pmax x1, blocking collectives, per_device(): top_max = lax.pmax(seq_max, ('page', 'tensor'))  66.4 us
    psum x1, blocking collectives, per_device(): lax.psum((seq_total * rescale, seq_acc * rescale[..., None]), ('page', 't...  65.2 us
    ppermute x7, starting transfers between devices, per_device(): lax.ppermute(extra[-1] if extra else query, axis_name='tensor', perm=trail)  38.2 us
    slice x1, local copies, waits for them, and re-layouts, per_device(): val_rows = pool_five[:, :, :, 1]  33.6 us
    scatter x1, local copies, waits for them, and re-layouts, per_device(): logical = jnp.zeros((pool_size,), jnp.int32).at[page_table].set(jnp.arang...  30.5 us
    reshape x1, local copies, waits for them, and re-layouts, per_device(): pool_five = kv_pool.reshape(slots, PAGE_TOK, KVH, 2, HD)  27.4 us
  transfers between devices with their start and end apart: 17, of which 10 were waited for; matrix products, arithmetic and copies ran while one was open for 19% of the time, Pallas kernels for 0%

profile of v1, /device:TPU:0, one launch (start us, length us, event | category | flops | bytes accessed | tf_op | source)
XLA Modules:
  0.0 516.4 jit_solution(14443161250811185182)
XLA Ops:
  8.0 24.1 %all-gather = bf16[1,32,1024]{2,0,1:T(2,128)(2,1)S(1)} all-gather(bf16[1,2,1024]{2,0,1:T(2,128)(2,1)S(1)} %copy.38), channel_id=2, replica_groups=mesh['page'=8,'tensor'=16] {'tensor'}, dimensions={1}, use_global_device_ids=true | all-gather | bytes 69632 | tf_op jit(solution)/shard_map/all_gather | solution.py:90
  32.1 2.3 fusion.12
  34.5 27.4 %reshape.161 = bf16[64,64,8,2,128]{4,3,2,1,0:T(2,128)(2,1)} reshape(bf16[64,64,2048]{2,1,0:T(8,128)(2,1)} %param.11) | data formatting | bytes 33554432 | tf_op jit(solution)/shard_map/reshape | solution.py:83
  61.9 33.6 %fusion.39 = (bf16[64,64,8,1,128]{4,3,2,1,0:T(2,128)(2,1)}, bf16[64,64,8,1,128]{4,3,2,1,0:T(2,128)(2,1)}) fusion(bf16[64,64,8,2,128]{4,3,2,1,0:T(2,128)(2,1)} %reshape.161), kind=kLoop, calls=%fused_computation.98 | loop fusion | bytes 33554432 | tf_op jit(solution)/shard_map/slice | solution.py:85
  95.5 30.5 %scatter_custom_fusion = s32[8192]{0:T(1024)S(1)} fusion(s32[8192]{0:T(1024)S(1)} %compare_select_fusion, s32[8192]{0:T(1024)S(1)} %iota.34, s32[]{:T(128)} %constant.95.clone.1), kind=kCustom, calls=%fused_computation.63 | custom fusion | bytes 32772 | tf_op jit(solution)/shard_map/scatter | solution.py:72
  127.1 1.3 collective-permute-start
  128.5 6.0 %collective-permute-done = bf16[32,512]{1,0:T(8,128)(2,1)S(1)} collective-permute-done((bf16[32,512]{1,0:T(8,128)(2,1)S(1)}, bf16[32,512]{1,0:T(8,128)(2,1)S(1)}, u32[]{:S(2)}, u32[]{:S(2)}) %collective-permute-start) | collective-permute-done | bytes 32800 | tf_op jit(solution)/shard_map/ppermute | solution.py:105
  134.6 5.4 %collective-permute-start.8 = (bf16[32,512]{1,0:T(8,128)(2,1)S(1)}, bf16[32,512]{1,0:T(8,128)(2,1)S(1)}, u32[]{:S(2)}, u32[]{:S(2)}) collective-permute-start(bf16[32,512]{1,0:T(8,128)(2,1)S(1)} %bitcast.114), channel_id=1, source_target_pairs={{1,0},{2,1},{3,2},{4,3},{5,4},{6,5},{7,6},{8,7},{9,8},{10,9},{11,1... | collective-permute-start | bytes 98312 | tf_op jit(solution)/shard_map/ppermute | solution.py:109
  140.0 1.7 collective-permute-done.1
  142.4 5.3 %collective-permute-start.9 = (bf16[32,512]{1,0:T(8,128)(2,1)S(1)}, bf16[32,512]{1,0:T(8,128)(2,1)S(1)}, u32[]{:S(2)}, u32[]{:S(2)}) collective-permute-start(bf16[32,512]{1,0:T(8,128)(2,1)S(1)} %collective-permute-done.8), channel_id=1, source_target_pairs={{1,0},{2,1},{3,2},{4,3},{5,4},{6,5},{7,6},{8,7},{9,8},{10,9},{11,1... | collective-permute-start | bytes 98312 | tf_op jit(solution)/shard_map/ppermute | solution.py:109
  147.7 1.3 collective-permute-done.2
  149.7 5.4 %collective-permute-start.10 = (bf16[32,512]{1,0:T(8,128)(2,1)S(1)}, bf16[32,512]{1,0:T(8,128)(2,1)S(1)}, u32[]{:S(2)}, u32[]{:S(2)}) collective-permute-start(bf16[32,512]{1,0:T(8,128)(2,1)S(1)} %collective-permute-done.9), channel_id=1, source_target_pairs={{1,0},{2,1},{3,2},{4,3},{5,4},{6,5},{7,6},{8,7},{9,8},{10,9},{11,1... | collective-permute-start | bytes 98312 | tf_op jit(solution)/shard_map/ppermute | solution.py:109
  155.1 1.1 collective-permute-done.3
  156.2 1.3 compare_reduce_fusion
  157.5 5.4 %collective-permute-start.11 = (bf16[32,512]{1,0:T(8,128)(2,1)S(1)}, bf16[32,512]{1,0:T(8,128)(2,1)S(1)}, u32[]{:S(2)}, u32[]{:S(2)}) collective-permute-start(bf16[32,512]{1,0:T(8,128)(2,1)S(1)} %collective-permute-done.10), channel_id=1, source_target_pairs={{1,0},{2,1},{3,2},{4,3},{5,4},{6,5},{7,6},{8,7},{9,8},{10,9},{11,1... | collective-permute-start | bytes 98312 | tf_op jit(solution)/shard_map/ppermute | solution.py:109
  164.5 5.6 %collective-permute-start.12 = (bf16[32,512]{1,0:T(8,128)(2,1)S(1)}, bf16[32,512]{1,0:T(8,128)(2,1)S(1)}, u32[]{:S(2)}, u32[]{:S(2)}) collective-permute-start(bf16[32,512]{1,0:T(8,128)(2,1)S(1)} %collective-permute-done.11), channel_id=1, source_target_pairs={{1,0},{2,1},{3,2},{4,3},{5,4},{6,5},{7,6},{8,7},{9,8},{10,9},{11,1... | collective-permute-start | bytes 98312 | tf_op jit(solution)/shard_map/ppermute | solution.py:109
  172.6 5.4 %collective-permute-start.13 = (bf16[32,512]{1,0:T(8,128)(2,1)S(1)}, bf16[32,512]{1,0:T(8,128)(2,1)S(1)}, u32[]{:S(2)}, u32[]{:S(2)}) collective-permute-start(bf16[32,512]{1,0:T(8,128)(2,1)S(1)} %collective-permute-done.12), channel_id=1, source_target_pairs={{1,0},{2,1},{3,2},{4,3},{5,4},{6,5},{7,6},{8,7},{9,8},{10,9},{11,1... | collective-permute-start | bytes 98312 | tf_op jit(solution)/shard_map/ppermute | solution.py:109
  179.6 5.6 %collective-permute-start.14 = (bf16[32,512]{1,0:T(8,128)(2,1)S(1)}, bf16[32,512]{1,0:T(8,128)(2,1)S(1)}, u32[]{:S(2)}, u32[]{:S(2)}) collective-permute-start(bf16[32,512]{1,0:T(8,128)(2,1)S(1)} %collective-permute-done.13), channel_id=1, source_target_pairs={{1,0},{2,1},{3,2},{4,3},{5,4},{6,5},{7,6},{8,7},{9,8},{10,9},{11,1... | collective-permute-start | bytes 98312 | tf_op jit(solution)/shard_map/ppermute | solution.py:109
  185.4 1.4 collective-permute-done.14
  187.4 1.2 gather_fusion.1
  188.9 10.3 %multiply_reduce_fusion = (f32[64,8,8]{2,1,0:T(8,128)S(1)}, f32[64,8,8,64]{3,2,1,0:T(8,128)S(1)}) fusion(bf16[64,8,8,128]{3,2,1,0:T(8,128)(2,1)S(1)} %bitcast.106, bf16[64,64,8,1,128]{4,3,2,1,0:T(2,128)(2,1)} %get-tuple-element.9), kind=kOutput, calls=%fused_computation.16 | convolution fusion | flops 67629056 | bytes 10502144 | tf_op jit(solution)/shard_map/sghd,stgd->sght/dot_general | solution.py:120
  200.1 1.7 copy.42
  203.6 1.4 gather_fusion.3
  205.0 2.0 convert_reduce_fusion
  207.1 66.4 %pmax.7 = f32[32,64]{0,1:T(8,128)S(1)} all-reduce(f32[32,64]{0,1:T(8,128)S(1)} %bitcast.111), channel_id=1, replica_groups=mesh['page'=8,'tensor'=16] {'page','tensor'}, use_global_device_ids=true, to_apply=%region_5.6 | all-reduce | flops 2048 | bytes 16384 | tf_op jit(solution)/shard_map/pmax | solution.py:143
  273.5 2.0 multiply_multiply_fusion.1
  275.5 9.7 %multiply_multiply_fusion = f32[64,8,8,128]{3,2,1,0:T(8,128)S(1)} fusion(bf16[64,64,8,1,128]{4,3,2,1,0:T(2,128)(2,1)} %get-tuple-element.8, f32[64,8,8]{2,1,0:T(8,128)S(1)} %get-tuple-element.3, f32[64,8]{1,0:T(8,128)} %convert_element_type.47, f32[64,8,8,64]{3,2,1,0:T(8,128)S(1)} %get-tuple-element.15, f32[64,8,8]{2,1,0:T(8,128)S(1)} %get-tuple-element.14), kind=kOutput, calls=%fused_computation.14 | convolution fusion | flops 68943872 | bytes 11569152 | tf_op jit(solution)/shard_map/sght,stgd->sghd/dot_general | solution.py:128
  285.2 3.1 fusion.5
  290.1 65.2 %psum.23 = f32[32,64]{0,1:T(8,128)S(1)} all-reduce(f32[32,64]{0,1:T(8,128)S(1)} %convolution_multiply_fusion), channel_id=1, replica_groups=mesh['page'=8,'tensor'=16] {'page','tensor'}, use_global_device_ids=true, to_apply=%region_8.9 | all-reduce | flops 2048 | bytes 16384 | tf_op jit(solution)/shard_map/psum | solution.py:145
  355.3 78.5 %all-reduce.7.cloned.1.call-done = f32[32,64,128]{2,0,1:T(8,128)} async-done(((f32[32,64,128]{2,0,1:T(8,128)}), f32[32,64,128]{2,0,1:T(8,128)}) %all-reduce.7.cloned.1.call-update) | async-done | bytes 1048592 | tf_op jit(solution)/shard_map/psum | solution.py:145
  433.9 1.2 fusion.17
  435.0 73.9 %all-reduce.8 = bf16[32,1024]{1,0:T(8,128)(2,1)S(1)} all-reduce(f32[32,1024]{1,0:T(8,128)S(1)} %fusion.17), channel_id=3, replica_groups=mesh['page'=8,'tensor'=16] {'tensor'}, use_global_device_ids=true, to_apply=%region_9.10.clone | all-reduce | flops 32768 | bytes 196608
  (102 shorter events, 14.4 us)
Async XLA Ops:
  7.2 426.7 %copy-start = (bf16[512,1024]{1,0:T(8,128)(2,1)S(1)}, bf16[512,1024]{1,0:T(8,128)(2,1)}, u32[]{:S(2)}) copy-start(bf16[512,1024]{1,0:T(8,128)(2,1)} %param.10) | copy-start | bytes 3145732
  7.2 27.3 %copy-start.6 = (s32[8192]{0:T(1024)S(1)}, s32[8192]{0:T(1024)}, u32[]{:S(2)}) copy-start(s32[8192]{0:T(1024)} %param.12) | copy-start | bytes 98308
  7.2 118.8 %all-reduce.5.cloned.1.call-start = ((), (), s32[]{:S(2)}) async-start(), calls=%async_computation | async-start | bytes 163840 | tf_op jit(solution)/shard_map/psum | solution.py:94
  34.4 399.5 %all-reduce.7.cloned.1.call-start = ((), (), s32[]{:S(2)}) async-start(), calls=%async_computation.1 | async-start | bytes 2097152 | tf_op jit(solution)/shard_map/psum | solution.py:145
  61.9 87.2 %copy-start.2 = (s32[1,32,8,32]{3,2,1,0:T(8,128)S(1)}, s32[1,32,8,32]{3,2,1,0:T(8,128)}, u32[]{:S(2)}) copy-start(s32[1,32,8,32]{3,2,1,0:T(8,128)} %param.13) | copy-start | bytes 98308
  61.9 109.5 %copy-start.14 = (u32[128]{0:T(128)S(1)}, u32[128]{0:T(128)}, u32[]{:S(2)}) copy-start(u32[128]{0:T(128)} %constant.134) | copy-start | bytes 1540
  95.5 39.0 %copy-start.10 = (f32[64]{0:T(128)}, f32[64]{0:T(128)S(1)}, u32[]{:S(2)}) copy-start(f32[64]{0:T(128)S(1)} %get-tuple-element.16) | copy-start | bytes 772
  95.5 53.5 %copy-start.12 = (f32[64]{0:T(128)}, f32[64]{0:T(128)S(1)}, u32[]{:S(2)}) copy-start(f32[64]{0:T(128)S(1)} %get-tuple-element.17) | copy-start | bytes 772
  127.1 7.4 %collective-permute-start = (bf16[32,512]{1,0:T(8,128)(2,1)S(1)}, bf16[32,512]{1,0:T(8,128)(2,1)S(1)}, u32[]{:S(2)}, u32[]{:S(2)}) collective-permute-start(bf16[32,512]{1,0:T(8,128)(2,1)S(1)} %bitcast.113), channel_id=1, source_target_pairs={{0,1},{1,2},{2,3},{3,4},{4,5},{5,6},{6,7},{7,8},{8,9},{9,10},{10,1... | collective-permute-start | bytes 98312 | tf_op jit(solution)/shard_map/ppermute | solution.py:105
  134.5 7.2 %collective-permute-start.1 = (bf16[32,512]{1,0:T(8,128)(2,1)S(1)}, bf16[32,512]{1,0:T(8,128)(2,1)S(1)}, u32[]{:S(2)}, u32[]{:S(2)}) collective-permute-start(bf16[32,512]{1,0:T(8,128)(2,1)S(1)} %collective-permute-done), channel_id=1, source_target_pairs={{0,1},{1,2},{2,3},{3,4},{4,5},{5,6},{6,7},{7,8},{8,9},{9,10},{10,1... | collective-permute-start | bytes 98312 | tf_op jit(solution)/shard_map/ppermute | solution.py:105
  134.6 14.4 %copy-start.7 = (s32[64]{0:T(128)}, s32[64]{0:T(128)S(1)}, u32[]{:S(2)}) copy-start(s32[64]{0:T(128)S(1)} %get-tuple-element.7) | copy-start | bytes 772
  134.6 7.8 %collective-permute-start.8 = (bf16[32,512]{1,0:T(8,128)(2,1)S(1)}, bf16[32,512]{1,0:T(8,128)(2,1)S(1)}, u32[]{:S(2)}, u32[]{:S(2)}) collective-permute-start(bf16[32,512]{1,0:T(8,128)(2,1)S(1)} %bitcast.114), channel_id=1, source_target_pairs={{1,0},{2,1},{3,2},{4,3},{5,4},{6,5},{7,6},{8,7},{9,8},{10,9},{11,1... | collective-permute-start | bytes 98312 | tf_op jit(solution)/shard_map/ppermute | solution.py:109
  141.8 7.2 %collective-permute-start.2 = (bf16[32,512]{1,0:T(8,128)(2,1)S(1)}, bf16[32,512]{1,0:T(8,128)(2,1)S(1)}, u32[]{:S(2)}, u32[]{:S(2)}) collective-permute-start(bf16[32,512]{1,0:T(8,128)(2,1)S(1)} %collective-permute-done.1), channel_id=1, source_target_pairs={{0,1},{1,2},{2,3},{3,4},{4,5},{5,6},{6,7},{7,8},{8,9},{9,10},{10,1... | collective-permute-start | bytes 98312 | tf_op jit(solution)/shard_map/ppermute | solution.py:105
  142.4 7.3 %collective-permute-start.9 = (bf16[32,512]{1,0:T(8,128)(2,1)S(1)}, bf16[32,512]{1,0:T(8,128)(2,1)S(1)}, u32[]{:S(2)}, u32[]{:S(2)}) collective-permute-start(bf16[32,512]{1,0:T(8,128)(2,1)S(1)} %collective-permute-done.8), channel_id=1, source_target_pairs={{1,0},{2,1},{3,2},{4,3},{5,4},{6,5},{7,6},{8,7},{9,8},{10,9},{11,1... | collective-permute-start | bytes 98312 | tf_op jit(solution)/shard_map/ppermute | solution.py:109
  149.0 7.2 %collective-permute-start.3 = (bf16[32,512]{1,0:T(8,128)(2,1)S(1)}, bf16[32,512]{1,0:T(8,128)(2,1)S(1)}, u32[]{:S(2)}, u32[]{:S(2)}) collective-permute-start(bf16[32,512]{1,0:T(8,128)(2,1)S(1)} %collective-permute-done.2), channel_id=1, source_target_pairs={{0,1},{1,2},{2,3},{3,4},{4,5},{5,6},{6,7},{7,8},{8,9},{9,10},{10,1... | collective-permute-start | bytes 98312 | tf_op jit(solution)/shard_map/ppermute | solution.py:105
  149.0 39.6 %copy-start.9 = (s32[1024]{0:T(1024)}, s32[1024]{0:T(1024)S(1)}, u32[]{:S(2)}) copy-start(s32[1024]{0:T(1024)S(1)} %pad_clamp_fusion) | copy-start | bytes 12292
  149.7 7.8 %collective-permute-start.10 = (bf16[32,512]{1,0:T(8,128)(2,1)S(1)}, bf16[32,512]{1,0:T(8,128)(2,1)S(1)}, u32[]{:S(2)}, u32[]{:S(2)}) collective-permute-start(bf16[32,512]{1,0:T(8,128)(2,1)S(1)} %collective-permute-done.9), channel_id=1, source_target_pairs={{1,0},{2,1},{3,2},{4,3},{5,4},{6,5},{7,6},{8,7},{9,8},{10,9},{11,1... | collective-permute-start | bytes 98312 | tf_op jit(solution)/shard_map/ppermute | solution.py:109
  156.2 7.2 %collective-permute-start.4 = (bf16[32,512]{1,0:T(8,128)(2,1)S(1)}, bf16[32,512]{1,0:T(8,128)(2,1)S(1)}, u32[]{:S(2)}, u32[]{:S(2)}) collective-permute-start(bf16[32,512]{1,0:T(8,128)(2,1)S(1)} %collective-permute-done.3), channel_id=1, source_target_pairs={{0,1},{1,2},{2,3},{3,4},{4,5},{5,6},{6,7},{7,8},{8,9},{9,10},{10,1... | collective-permute-start | bytes 98312 | tf_op jit(solution)/shard_map/ppermute | solution.py:105
  157.5 41.8 %copy-start.4 = (pred[64,8]{1,0:T(8,128)(4,1)}, pred[64,8]{1,0:T(8,128)(4,1)S(1)}, u32[]{:S(2)}) copy-start(pred[64,8]{1,0:T(8,128)(4,1)S(1)} %compare_reduce_fusion) | copy-start | bytes 1540
  157.5 7.0 %collective-permute-start.11 = (bf16[32,512]{1,0:T(8,128)(2,1)S(1)}, bf16[32,512]{1,0:T(8,128)(2,1)S(1)}, u32[]{:S(2)}, u32[]{:S(2)}) collective-permute-start(bf16[32,512]{1,0:T(8,128)(2,1)S(1)} %collective-permute-done.10), channel_id=1, source_target_pairs={{1,0},{2,1},{3,2},{4,3},{5,4},{6,5},{7,6},{8,7},{9,8},{10,9},{11,1... | collective-permute-start | bytes 98312 | tf_op jit(solution)/shard_map/ppermute | solution.py:109
  163.5 7.2 %collective-permute-start.5 = (bf16[32,512]{1,0:T(8,128)(2,1)S(1)}, bf16[32,512]{1,0:T(8,128)(2,1)S(1)}, u32[]{:S(2)}, u32[]{:S(2)}) collective-permute-start(bf16[32,512]{1,0:T(8,128)(2,1)S(1)} %collective-permute-done.4), channel_id=1, source_target_pairs={{0,1},{1,2},{2,3},{3,4},{4,5},{5,6},{6,7},{7,8},{8,9},{9,10},{10,1... | collective-permute-start | bytes 98312 | tf_op jit(solution)/shard_map/ppermute | solution.py:105
  164.5 8.1 %collective-permute-start.12 = (bf16[32,512]{1,0:T(8,128)(2,1)S(1)}, bf16[32,512]{1,0:T(8,128)(2,1)S(1)}, u32[]{:S(2)}, u32[]{:S(2)}) collective-permute-start(bf16[32,512]{1,0:T(8,128)(2,1)S(1)} %collective-permute-done.11), channel_id=1, source_target_pairs={{1,0},{2,1},{3,2},{4,3},{5,4},{6,5},{7,6},{8,7},{9,8},{10,9},{11,1... | collective-permute-start | bytes 98312 | tf_op jit(solution)/shard_map/ppermute | solution.py:109
  170.7 7.3 %collective-permute-start.6 = (bf16[32,512]{1,0:T(8,128)(2,1)S(1)}, bf16[32,512]{1,0:T(8,128)(2,1)S(1)}, u32[]{:S(2)}, u32[]{:S(2)}) collective-permute-start(bf16[32,512]{1,0:T(8,128)(2,1)S(1)} %collective-permute-done.5), channel_id=1, source_target_pairs={{0,1},{1,2},{2,3},{3,4},{4,5},{5,6},{6,7},{7,8},{8,9},{9,10},{10,1... | collective-permute-start | bytes 98312 | tf_op jit(solution)/shard_map/ppermute | solution.py:105
  172.6 7.0 %collective-permute-start.13 = (bf16[32,512]{1,0:T(8,128)(2,1)S(1)}, bf16[32,512]{1,0:T(8,128)(2,1)S(1)}, u32[]{:S(2)}, u32[]{:S(2)}) collective-permute-start(bf16[32,512]{1,0:T(8,128)(2,1)S(1)} %collective-permute-done.12), channel_id=1, source_target_pairs={{1,0},{2,1},{3,2},{4,3},{5,4},{6,5},{7,6},{8,7},{9,8},{10,9},{11,1... | collective-permute-start | bytes 98312 | tf_op jit(solution)/shard_map/ppermute | solution.py:109
  178.0 7.2 %collective-permute-start.7 = (bf16[32,512]{1,0:T(8,128)(2,1)S(1)}, bf16[32,512]{1,0:T(8,128)(2,1)S(1)}, u32[]{:S(2)}, u32[]{:S(2)}) collective-permute-start(bf16[32,512]{1,0:T(8,128)(2,1)S(1)} %collective-permute-done.6), channel_id=1, source_target_pairs={{0,1},{1,2},{2,3},{3,4},{4,5},{5,6},{6,7},{7,8},{8,9},{9,10},{10,1... | collective-permute-start | bytes 98312 | tf_op jit(solution)/shard_map/ppermute | solution.py:105
  179.6 7.2 %collective-permute-start.14 = (bf16[32,512]{1,0:T(8,128)(2,1)S(1)}, bf16[32,512]{1,0:T(8,128)(2,1)S(1)}, u32[]{:S(2)}, u32[]{:S(2)}) collective-permute-start(bf16[32,512]{1,0:T(8,128)(2,1)S(1)} %collective-permute-done.13), channel_id=1, source_target_pairs={{1,0},{2,1},{3,2},{4,3},{5,4},{6,5},{7,6},{8,7},{9,8},{10,9},{11,1... | collective-permute-start | bytes 98312 | tf_op jit(solution)/shard_map/ppermute | solution.py:109
  205.0 2.0 copy-start.3
  205.0 68.5 %copy-start.5 = (pred[64,8]{1,0:T(8,128)(4,1)S(1)}, pred[64,8]{1,0:T(8,128)(4,1)}, u32[]{:S(2)}) copy-start(pred[64,8]{1,0:T(8,128)(4,1)} %copy-done.4) | copy-start | bytes 1540
  275.5 9.7 %copy-start.8 = (s32[64]{0:T(128)S(1)}, s32[64]{0:T(128)}, u32[]{:S(2)}) copy-start(s32[64]{0:T(128)} %copy-done.7) | copy-start | bytes 772
  285.2 3.2 copy-start.11
  285.2 3.2 copy-start.13
  285.2 4.6 copy-start.1
Sparse Core Ops, SparseCore 0:
  34.5 55.7 all-reduce.4
  288.5 145.3 all-reduce.6
